TPU v7x, 32 devices: a whole 2x2x4 slice. The times are simulated.
32 devices in a mesh: circ: 4 (over z), normal: 2 (over y), span: 4 (over x, core).
Axes of the slice: x: 2, y: 2, z: 4, core: 2. Of those that a mesh axis runs over, the one named last changes fastest.
Arguments:
- adjoint: float32 [5, 16, 32, 512], P(None, 'span', 'normal', 'circ'), may hold values from -6 to 6
- objective_grad: float32 [5, 16, 32, 512], P(None, 'span', 'normal', 'circ'), may hold values from -6 to 6
- face_weights: float32 [3, 16, 32, 512], P(None, 'span', 'normal', 'circ'), may hold values from 0.2 to 2
- owner_jac: float32 [3, 5, 5], replicated, may hold values from -2.5 to 2.5
- neighbor_jac: float32 [3, 5, 5], replicated, may hold values from -2.5 to 2.5
- coupling: float32 [3, 5], replicated, may hold values from -2.5 to 2.5
- stiffness: float32 [16, 32, 512], P('span', 'normal', 'circ'), may hold values from 0.3 to 3
- wall_kernel: float32 [16, 32, 512], P('span', 'normal', 'circ'), may hold values from -0.25 to 0.25
- panel_owner: int32 [16, 512], P('span', 'circ'), may hold values from 0 to 511, as said below
Outputs:
- adjoint_residual: float32 [5, 16, 32, 512], P(None, 'span', 'normal', 'circ')
- mesh_adjoint: float32 [3, 16, 32, 512], P(None, 'span', 'normal', 'circ')
- panel_sens: float32 [3, 512], P(None, 'span')
Inputs may be any that keep to these rules, and one draw needn't show every extreme that they name: `panel_owner`: the panel of a wall face at station k is owned by span index k // 4 or the one beside it; panels hold ragged numbers of faces.
All inputs are finite; a program needn't handle non-finite values.
Results may differ from a plain program's by a relative error of at most 0.00011.
Values sent between devices are 32-bit elements; how exact they have to be, the bound alone decides.
No kernel may reach another device: no remote copies, remote signals or barrier semaphores. Data moves between devices by JAX's collectives and lax.ppermute only.
A program may use at most 64 MiB of HBM per device.

v0:
```python
import jax
import jax.numpy as jnp
from jax import lax
from jax.sharding import PartitionSpec as P

PANEL_DEV = 128
SWEEPS = 4


def padded_2(array, sides, width, wrap):
    for axis, dim in sides:
        peers, length = (lax.axis_size(axis), array.shape[dim])
        up = [(i, (i + 1) % peers) for i in range(peers if wrap else peers - 1)]
        down = [(j, i) for i, j in up]
        last = lax.slice_in_dim(array, length - width, length, axis=dim)
        initial = lax.slice_in_dim(array, 0, width, axis=dim)
        before = lax.ppermute(last, axis, up)
        after = lax.ppermute(initial, axis, down)
        array = jnp.concatenate([before, array, after], axis=dim)
    return array


def neighbor_sum(padded):
    total = padded[:, 2:, 1:-1, 1:-1] + padded[:, :-2, 1:-1, 1:-1]
    total = total + padded[:, 1:-1, 2:, 1:-1] + padded[:, 1:-1, :-2, 1:-1]
    return total + padded[:, 1:-1, 1:-1, 2:] + padded[:, 1:-1, 1:-1, :-2]


def inner(field):
    return field[:, 1:-1, 1:-1, 1:-1]


def flux_transpose(padded, owner_jac, neighbor_jac):
    psi = padded[:5]
    weights = padded[5:]
    center = inner(psi)
    total = jnp.zeros_like(center)
    for direction in range(3):
        lower = [slice(None), slice(1, -1), slice(1, -1), slice(1, -1)]
        upper = [slice(None), slice(1, -1), slice(1, -1), slice(1, -1)]
        lower[direction + 1] = slice(0, -2)
        upper[direction + 1] = slice(2, None)
        w_here = weights[direction, 1:-1, 1:-1, 1:-1]
        w_lower = weights[direction][tuple(lower[1:])]
        up_term = w_here[None] * (center - psi[tuple(upper)])
        down_term = w_lower[None] * (psi[tuple(lower)] - center)
        total = total + jnp.einsum(
            "uv,ukji->vkji", owner_jac[direction], up_term, precision=lax.Precision.HIGHEST
        )
        total = total + jnp.einsum(
            "uv,ukji->vkji", neighbor_jac[direction], down_term, precision=lax.Precision.HIGHEST
        )
    return total


def relax(mesh_pad, stiff_pad, force_pad):
    weighted = stiff_pad[None] * mesh_pad
    stiff_in = stiff_pad[1:-1, 1:-1, 1:-1]
    diag_term = 6.0 * stiff_in + 1.0
    mesh_in = inner(mesh_pad)
    return (
        mesh_in
        + 0.8
        * (inner(force_pad) - diag_term[None] * mesh_in + neighbor_sum(weighted))
        / diag_term[None]
    )


def run_sweeps(stiff_pad, force_pad):
    mesh_pad = 0.8 * force_pad / (6.0 * stiff_pad[None] + 1.0)
    for sweep in range(1, SWEEPS):
        mesh_pad = relax(mesh_pad, stiff_pad, force_pad)
        stiff_pad = stiff_pad[1:-1, 1:-1, 1:-1]
        force_pad = inner(force_pad)
    return mesh_pad


def on_device(
    adjoint,
    objective_grad,
    face_weights,
    owner_jac,
    neighbor_jac,
    coupling,
    stiffness,
    wall_kernel,
    panel_owner,
):
    stacked = jnp.concatenate([adjoint, face_weights], axis=0)
    beside_all = padded_2(stacked, (("circ", 3),), 1, True)
    padded = padded_2(beside_all, (("normal", 2), ("span", 1)), 1, False)
    residual = flux_transpose(padded, owner_jac, neighbor_jac) + adjoint - objective_grad
    forcing = jnp.einsum("mv,vkji->mkji", coupling, residual, precision=lax.Precision.HIGHEST)
    margin = SWEEPS - 1
    joined = jnp.concatenate([stiffness[None], forcing], axis=0)
    cycle_pad = padded_2(joined, (("circ", 3),), margin, True)
    full_pad = padded_2(cycle_pad, (("normal", 2), ("span", 1)), margin, False)
    mesh = run_sweeps(full_pad[0], full_pad[1:])
    wall_sens = jnp.sum(wall_kernel[None] * mesh, axis=2)
    panel_count = PANEL_DEV * lax.axis_size("span")
    onehot = (
        panel_owner[:, :, None] == jnp.arange(panel_count, dtype=jnp.int32)[None, None, :]
    ).astype(jnp.float32)
    terms = jnp.einsum("mki,kip->mp", wall_sens, onehot, precision=lax.Precision.HIGHEST)
    total = lax.psum(terms, ("circ", "normal", "span"))
    panels = lax.dynamic_slice_in_dim(total, lax.axis_index("span") * PANEL_DEV, PANEL_DEV, 1)
    return (residual, mesh, panels)


def solution(mesh):
    placed = (
        P(None, "span", "normal", "circ"),
        P(None, "span", "normal", "circ"),
        P(None, "span", "normal", "circ"),
        P(),
        P(),
        P(),
        P("span", "normal", "circ"),
        P("span", "normal", "circ"),
        P("span", "circ"),
    )
    return jax.shard_map(
        on_device,
        mesh=mesh,
        in_specs=placed,
        out_specs=(
            P(None, "span", "normal", "circ"),
            P(None, "span", "normal", "circ"),
            P(None, "span"),
        ),
        check_vma=False,
    )
```

profile of v0, /device:TPU:14, one launch (start us, length us, event | category | flops | bytes accessed | tf_op | source)
XLA Modules:
  0.0 115.0 jit_solution(1528439476088058492)
XLA Ops:
  0.7 1.0 constant_dynamic-update-slice_fusion.1
  1.8 1.6 %collective-permute-start = (f32[8,4,16,1]{3,2,1,0:T(8,128)S(1)}, f32[8,4,16,1]{3,2,1,0:T(8,128)S(1)}, u32[]{:S(2)}, u32[]{:S(2)}) collective-permute-start(f32[8,4,16,1]{3,2,1,0:T(8,128)S(1)} %get-tuple-element.32), channel_id=1, source_target_pairs={{0,8},{8,16},{16,24},{24,0},{1,9},{9,17},{17,25},{25,1},{2,10},{10... | collective-permute-start | bytes 6152 | tf_op jit(solution)/shard_map/ppermute | solution.py:17
  3.9 7.2 %collective-permute-done = f32[8,4,16,1]{3,2,1,0:T(8,128)S(1)} collective-permute-done((f32[8,4,16,1]{3,2,1,0:T(8,128)S(1)}, f32[8,4,16,1]{3,2,1,0:T(8,128)S(1)}, u32[]{:S(2)}, u32[]{:S(2)}) %collective-permute-start) | collective-permute-done | bytes 2080 | tf_op jit(solution)/shard_map/ppermute | solution.py:17
  11.0 5.3 %collective-permute-done.1 = f32[8,4,16,1]{3,2,1,0:T(8,128)S(1)} collective-permute-done((f32[8,4,16,1]{3,2,1,0:T(8,128)S(1)}, f32[8,4,16,1]{3,2,1,0:T(8,128)S(1)}, u32[]{:S(2)}, u32[]{:S(2)}) %collective-permute-start.1) | collective-permute-done | bytes 2080 | tf_op jit(solution)/shard_map/ppermute | solution.py:18
  16.6 1.3 %collective-permute-start.2 = (f32[8,4,1,130]{3,2,1,0:T(1,128)S(1)}, f32[8,4,1,130]{3,2,1,0:T(1,128)S(1)}, u32[]{:S(2)}, u32[]{:S(2)}) collective-permute-start(f32[8,4,1,130]{3,2,1,0:T(1,128)S(1)} %get-tuple-element.24), channel_id=1, source_target_pairs={{0,4},{1,5},{2,6},{3,7},{8,12},{9,13},{10,14},{11,15},{16,20},{17,... | collective-permute-start | bytes 49928 | tf_op jit(solution)/shard_map/ppermute | solution.py:17
  17.9 4.5 %collective-permute-start.3 = (f32[8,4,1,130]{3,2,1,0:T(1,128)S(1)}, f32[8,4,1,130]{3,2,1,0:T(1,128)S(1)}, u32[]{:S(2)}, u32[]{:S(2)}) collective-permute-start(f32[8,4,1,130]{3,2,1,0:T(1,128)S(1)} %get-tuple-element.25), channel_id=1, source_target_pairs={{4,0},{5,1},{6,2},{7,3},{12,8},{13,9},{14,10},{15,11},{20,16},{21,... | collective-permute-start | bytes 49928 | tf_op jit(solution)/shard_map/ppermute | solution.py:18
  22.5 1.5 %collective-permute-done.3 = f32[8,4,1,130]{3,2,1,0:T(1,128)S(1)} collective-permute-done((f32[8,4,1,130]{3,2,1,0:T(1,128)S(1)}, f32[8,4,1,130]{3,2,1,0:T(1,128)S(1)}, u32[]{:S(2)}, u32[]{:S(2)}) %collective-permute-start.3) | collective-permute-done | bytes 16672 | tf_op jit(solution)/shard_map/ppermute | solution.py:18
  24.3 1.9 %collective-permute-start.5 = (f32[8,1,18,130]{3,2,1,0:T(8,128)S(1)}, f32[8,1,18,130]{3,2,1,0:T(8,128)S(1)}, u32[]{:S(2)}, u32[]{:S(2)}) collective-permute-start(f32[8,1,18,130]{3,2,1,0:T(8,128)S(1)} %get-tuple-element.22), channel_id=1, source_target_pairs={{0,1},{1,2},{2,3},{4,5},{5,6},{6,7},{8,9},{9,10},{10,11},{12,13},{... | collective-permute-start | bytes 224648 | tf_op jit(solution)/shard_map/ppermute | solution.py:17
  26.2 3.6 %collective-permute-start.4 = (f32[8,1,18,130]{3,2,1,0:T(8,128)S(1)}, f32[8,1,18,130]{3,2,1,0:T(8,128)S(1)}, u32[]{:S(2)}, u32[]{:S(2)}) collective-permute-start(f32[8,1,18,130]{3,2,1,0:T(8,128)S(1)} %get-tuple-element.23), channel_id=1, source_target_pairs={{1,0},{2,1},{3,2},{5,4},{6,5},{7,6},{9,8},{10,9},{11,10},{13,12},{... | collective-permute-start | bytes 224648 | tf_op jit(solution)/shard_map/ppermute | solution.py:18
  29.9 1.4 %collective-permute-done.5 = f32[8,1,18,130]{3,2,1,0:T(8,128)S(1)} collective-permute-done((f32[8,1,18,130]{3,2,1,0:T(8,128)S(1)}, f32[8,1,18,130]{3,2,1,0:T(8,128)S(1)}, u32[]{:S(2)}, u32[]{:S(2)}) %collective-permute-start.5) | collective-permute-done | bytes 74912 | tf_op jit(solution)/shard_map/ppermute | solution.py:17
  31.3 1.8 %collective-permute-done.4 = f32[8,1,18,130]{3,2,1,0:T(8,128)S(1)} collective-permute-done((f32[8,1,18,130]{3,2,1,0:T(8,128)S(1)}, f32[8,1,18,130]{3,2,1,0:T(8,128)S(1)}, u32[]{:S(2)}, u32[]{:S(2)}) %collective-permute-start.4) | collective-permute-done | bytes 74912 | tf_op jit(solution)/shard_map/ppermute | solution.py:18
  39.8 1.3 %collective-permute-start.7 = (f32[4,4,16,3]{3,0,2,1:T(4,128)S(1)}, f32[4,4,16,3]{3,0,2,1:T(4,128)S(1)}, u32[]{:S(2)}, u32[]{:S(2)}) collective-permute-start(f32[4,4,16,3]{3,0,2,1:T(4,128)S(1)} %get-tuple-element.39), channel_id=1, source_target_pairs={{8,0},{16,8},{24,16},{0,24},{9,1},{17,9},{25,17},{1,25},{10,2},{18... | collective-permute-start | bytes 9224 | tf_op jit(solution)/shard_map/ppermute | solution.py:18
  41.1 2.9 %collective-permute-done.6 = f32[4,4,16,3]{3,0,2,1:T(4,128)S(1)} collective-permute-done((f32[4,4,16,3]{3,0,2,1:T(4,128)S(1)}, f32[4,4,16,3]{3,0,2,1:T(4,128)S(1)}, u32[]{:S(2)}, u32[]{:S(2)}) %collective-permute-start.6) | collective-permute-done | bytes 3104 | tf_op jit(solution)/shard_map/ppermute | solution.py:17
  44.0 2.1 %collective-permute-done.7 = f32[4,4,16,3]{3,0,2,1:T(4,128)S(1)} collective-permute-done((f32[4,4,16,3]{3,0,2,1:T(4,128)S(1)}, f32[4,4,16,3]{3,0,2,1:T(4,128)S(1)}, u32[]{:S(2)}, u32[]{:S(2)}) %collective-permute-start.7) | collective-permute-done | bytes 3104 | tf_op jit(solution)/shard_map/ppermute | solution.py:18
  46.4 1.3 %collective-permute-start.8 = (f32[4,4,3,134]{3,0,2,1:T(4,128)S(1)}, f32[4,4,3,134]{3,0,2,1:T(4,128)S(1)}, u32[]{:S(2)}, u32[]{:S(2)}) collective-permute-start(f32[4,4,3,134]{3,0,2,1:T(4,128)S(1)} %get-tuple-element.28), channel_id=1, source_target_pairs={{0,4},{1,5},{2,6},{3,7},{8,12},{9,13},{10,14},{11,15},{16,20},{17,... | collective-permute-start | bytes 77192 | tf_op jit(solution)/shard_map/ppermute | solution.py:17
  47.7 4.5 %collective-permute-start.9 = (f32[4,4,3,134]{3,0,2,1:T(4,128)S(1)}, f32[4,4,3,134]{3,0,2,1:T(4,128)S(1)}, u32[]{:S(2)}, u32[]{:S(2)}) collective-permute-start(f32[4,4,3,134]{3,0,2,1:T(4,128)S(1)} %get-tuple-element.29), channel_id=1, source_target_pairs={{4,0},{5,1},{6,2},{7,3},{12,8},{13,9},{14,10},{15,11},{20,16},{21,... | collective-permute-start | bytes 77192 | tf_op jit(solution)/shard_map/ppermute | solution.py:18
  52.4 1.6 %collective-permute-done.9 = f32[4,4,3,134]{3,0,2,1:T(4,128)S(1)} collective-permute-done((f32[4,4,3,134]{3,0,2,1:T(4,128)S(1)}, f32[4,4,3,134]{3,0,2,1:T(4,128)S(1)}, u32[]{:S(2)}, u32[]{:S(2)}) %collective-permute-start.9) | collective-permute-done | bytes 25760 | tf_op jit(solution)/shard_map/ppermute | solution.py:18
  54.4 1.9 %collective-permute-start.10 = (f32[4,3,22,134]{3,0,2,1:T(4,128)S(1)}, f32[4,3,22,134]{3,0,2,1:T(4,128)S(1)}, u32[]{:S(2)}, u32[]{:S(2)}) collective-permute-start(f32[4,3,22,134]{3,0,2,1:T(4,128)S(1)} %get-tuple-element.30), channel_id=1, source_target_pairs={{0,1},{1,2},{2,3},{4,5},{5,6},{6,7},{8,9},{9,10},{10,11},{12,13},{... | collective-permute-start | bytes 424520 | tf_op jit(solution)/shard_map/ppermute | solution.py:17
  56.4 3.8 %collective-permute-start.11 = (f32[4,3,22,134]{3,0,2,1:T(4,128)S(1)}, f32[4,3,22,134]{3,0,2,1:T(4,128)S(1)}, u32[]{:S(2)}, u32[]{:S(2)}) collective-permute-start(f32[4,3,22,134]{3,0,2,1:T(4,128)S(1)} %get-tuple-element.31), channel_id=1, source_target_pairs={{1,0},{2,1},{3,2},{5,4},{6,5},{7,6},{9,8},{10,9},{11,10},{13,12},{... | collective-permute-start | bytes 424520 | tf_op jit(solution)/shard_map/ppermute | solution.py:18
  60.9 1.3 %collective-permute-done.10 = f32[4,3,22,134]{3,0,2,1:T(4,128)S(1)} collective-permute-done((f32[4,3,22,134]{3,0,2,1:T(4,128)S(1)}, f32[4,3,22,134]{3,0,2,1:T(4,128)S(1)}, u32[]{:S(2)}, u32[]{:S(2)}) %collective-permute-start.10) | collective-permute-done | bytes 141536 | tf_op jit(solution)/shard_map/ppermute | solution.py:17
  62.2 1.8 %collective-permute-done.11 = f32[4,3,22,134]{3,0,2,1:T(4,128)S(1)} collective-permute-done((f32[4,3,22,134]{3,0,2,1:T(4,128)S(1)}, f32[4,3,22,134]{3,0,2,1:T(4,128)S(1)}, u32[]{:S(2)}, u32[]{:S(2)}) %collective-permute-start.11) | collective-permute-done | bytes 141536 | tf_op jit(solution)/shard_map/ppermute | solution.py:18
  65.7 2.4 %broadcast_multiply_fusion.1 = (f32[3,8,20,132]{3,0,2,1:T(4,128)S(1)}, f32[3,8,20,132]{3,0,2,1:T(4,128)S(1)}) fusion(f32[8,20,132]{2,1,0:T(8,128)S(1)} %get-tuple-element.37, f32[3,10,22,134]{3,0,2,1:T(4,128)S(1)} %get-tuple-element.12, f32[8,20,132]{2,1,0:T(8,128)S(1)} %get-tuple-element.36, f32[4,10,22,134]{3,0,2,1:T(4,128)S(1)} %pad_maximum_fusion, ...), kind=kLoop, calls=%fused_computation.35 | loop fusion | flops 760320 | bytes 2703360 | tf_op jit(solution)/shard_map/mul | solution.py:57
  68.2 1.7 %broadcast_multiply_fusion.2 = (f32[3,6,18,130]{3,0,2,1:T(4,128)S(1)}, f32[3,6,18,130]{3,0,2,1:T(4,128)S(1)}) fusion(f32[6,18,130]{2,1,0:T(8,128)S(1)} %get-tuple-element.35, f32[3,8,20,132]{3,0,2,1:T(4,128)S(1)} %get-tuple-element.10, f32[6,18,130]{2,1,0:T(8,128)S(1)} %get-tuple-element.34, f32[4,10,22,134]{3,0,2,1:T(4,128)S(1)} %pad_maximum_fusion, ...), kind=kLoop, calls=%fused_computation.46 | loop fusion | flops 505440 | bytes 1797120 | tf_op jit(solution)/shard_map/mul | solution.py:57
  71.0 42.7 %psum.7 = f32[3,512]{1,0:T(4,128)S(1)} all-reduce(f32[3,512]{1,0:T(4,128)S(1)} %convolution_bitcast_fusion.1), channel_id=1, replica_groups=mesh['circ'=4,'normal'=2,'span'=4] {'circ','normal','span'}, use_global_device_ids=true, to_apply=%region_1.0 | all-reduce | flops 1536 | bytes 12288 | tf_op jit(solution)/shard_map/psum | solution.py:105
  (59 shorter events, 13.3 us)
Async XLA Ops:
  0.6 37.4 %copy-start = (f32[3,5]{1,0:T(4,128)S(1)}, f32[3,5]{1,0:T(4,128)}, u32[]{:S(2)}) copy-start(f32[3,5]{1,0:T(4,128)} %param.14) | copy-start | bytes 184
  0.6 1.0 copy-start.4
  1.8 9.2 %collective-permute-start = (f32[8,4,16,1]{3,2,1,0:T(8,128)S(1)}, f32[8,4,16,1]{3,2,1,0:T(8,128)S(1)}, u32[]{:S(2)}, u32[]{:S(2)}) collective-permute-start(f32[8,4,16,1]{3,2,1,0:T(8,128)S(1)} %get-tuple-element.32), channel_id=1, source_target_pairs={{0,8},{8,16},{16,24},{24,0},{1,9},{9,17},{17,25},{25,1},{2,10},{10... | collective-permute-start | bytes 6152 | tf_op jit(solution)/shard_map/ppermute | solution.py:17
  3.4 12.9 %collective-permute-start.1 = (f32[8,4,16,1]{3,2,1,0:T(8,128)S(1)}, f32[8,4,16,1]{3,2,1,0:T(8,128)S(1)}, u32[]{:S(2)}, u32[]{:S(2)}) collective-permute-start(f32[8,4,16,1]{3,2,1,0:T(8,128)S(1)} %get-tuple-element.33), channel_id=1, source_target_pairs={{8,0},{16,8},{24,16},{0,24},{9,1},{17,9},{25,17},{1,25},{10,2},{18... | collective-permute-start | bytes 6152 | tf_op jit(solution)/shard_map/ppermute | solution.py:18
  3.9 18.6 %copy-start.6 = (f32[3,5,5]{2,0,1:T(4,128)S(1)}, f32[3,5,5]{2,0,1:T(4,128)}, u32[]{:S(2)}) copy-start(f32[3,5,5]{2,0,1:T(4,128)} %param.12) | copy-start | bytes 904
  16.6 5.9 %collective-permute-start.2 = (f32[8,4,1,130]{3,2,1,0:T(1,128)S(1)}, f32[8,4,1,130]{3,2,1,0:T(1,128)S(1)}, u32[]{:S(2)}, u32[]{:S(2)}) collective-permute-start(f32[8,4,1,130]{3,2,1,0:T(1,128)S(1)} %get-tuple-element.24), channel_id=1, source_target_pairs={{0,4},{1,5},{2,6},{3,7},{8,12},{9,13},{10,14},{11,15},{16,20},{17,... | collective-permute-start | bytes 49928 | tf_op jit(solution)/shard_map/ppermute | solution.py:17
  17.9 6.1 %collective-permute-start.3 = (f32[8,4,1,130]{3,2,1,0:T(1,128)S(1)}, f32[8,4,1,130]{3,2,1,0:T(1,128)S(1)}, u32[]{:S(2)}, u32[]{:S(2)}) collective-permute-start(f32[8,4,1,130]{3,2,1,0:T(1,128)S(1)} %get-tuple-element.25), channel_id=1, source_target_pairs={{4,0},{5,1},{6,2},{7,3},{12,8},{13,9},{14,10},{15,11},{20,16},{21,... | collective-permute-start | bytes 49928 | tf_op jit(solution)/shard_map/ppermute | solution.py:18
  22.5 7.4 %copy-start.7 = (f32[3,5,5]{2,0,1:T(4,128)S(1)}, f32[3,5,5]{2,0,1:T(4,128)}, u32[]{:S(2)}) copy-start(f32[3,5,5]{2,0,1:T(4,128)} %param.13) | copy-start | bytes 904
  24.3 7.0 %collective-permute-start.5 = (f32[8,1,18,130]{3,2,1,0:T(8,128)S(1)}, f32[8,1,18,130]{3,2,1,0:T(8,128)S(1)}, u32[]{:S(2)}, u32[]{:S(2)}) collective-permute-start(f32[8,1,18,130]{3,2,1,0:T(8,128)S(1)} %get-tuple-element.22), channel_id=1, source_target_pairs={{0,1},{1,2},{2,3},{4,5},{5,6},{6,7},{8,9},{9,10},{10,11},{12,13},{... | collective-permute-start | bytes 224648 | tf_op jit(solution)/shard_map/ppermute | solution.py:17
  26.2 6.8 %collective-permute-start.4 = (f32[8,1,18,130]{3,2,1,0:T(8,128)S(1)}, f32[8,1,18,130]{3,2,1,0:T(8,128)S(1)}, u32[]{:S(2)}, u32[]{:S(2)}) collective-permute-start(f32[8,1,18,130]{3,2,1,0:T(8,128)S(1)} %get-tuple-element.23), channel_id=1, source_target_pairs={{1,0},{2,1},{3,2},{5,4},{6,5},{7,6},{9,8},{10,9},{11,10},{13,12},{... | collective-permute-start | bytes 224648 | tf_op jit(solution)/shard_map/ppermute | solution.py:18
  33.2 0.9 copy-start.1
  36.5 0.9 copy-start.3
  38.0 0.8 copy-start.2
  39.0 5.0 %collective-permute-start.6 = (f32[4,4,16,3]{3,0,2,1:T(4,128)S(1)}, f32[4,4,16,3]{3,0,2,1:T(4,128)S(1)}, u32[]{:S(2)}, u32[]{:S(2)}) collective-permute-start(f32[4,4,16,3]{3,0,2,1:T(4,128)S(1)} %get-tuple-element.38), channel_id=1, source_target_pairs={{0,8},{8,16},{16,24},{24,0},{1,9},{9,17},{17,25},{25,1},{2,10},{10... | collective-permute-start | bytes 9224 | tf_op jit(solution)/shard_map/ppermute | solution.py:17
  39.8 6.4 %collective-permute-start.7 = (f32[4,4,16,3]{3,0,2,1:T(4,128)S(1)}, f32[4,4,16,3]{3,0,2,1:T(4,128)S(1)}, u32[]{:S(2)}, u32[]{:S(2)}) collective-permute-start(f32[4,4,16,3]{3,0,2,1:T(4,128)S(1)} %get-tuple-element.39), channel_id=1, source_target_pairs={{8,0},{16,8},{24,16},{0,24},{9,1},{17,9},{25,17},{1,25},{10,2},{18... | collective-permute-start | bytes 9224 | tf_op jit(solution)/shard_map/ppermute | solution.py:18
  46.4 6.0 %collective-permute-start.8 = (f32[4,4,3,134]{3,0,2,1:T(4,128)S(1)}, f32[4,4,3,134]{3,0,2,1:T(4,128)S(1)}, u32[]{:S(2)}, u32[]{:S(2)}) collective-permute-start(f32[4,4,3,134]{3,0,2,1:T(4,128)S(1)} %get-tuple-element.28), channel_id=1, source_target_pairs={{0,4},{1,5},{2,6},{3,7},{8,12},{9,13},{10,14},{11,15},{16,20},{17,... | collective-permute-start | bytes 77192 | tf_op jit(solution)/shard_map/ppermute | solution.py:17
  47.7 6.3 %collective-permute-start.9 = (f32[4,4,3,134]{3,0,2,1:T(4,128)S(1)}, f32[4,4,3,134]{3,0,2,1:T(4,128)S(1)}, u32[]{:S(2)}, u32[]{:S(2)}) collective-permute-start(f32[4,4,3,134]{3,0,2,1:T(4,128)S(1)} %get-tuple-element.29), channel_id=1, source_target_pairs={{4,0},{5,1},{6,2},{7,3},{12,8},{13,9},{14,10},{15,11},{20,16},{21,... | collective-permute-start | bytes 77192 | tf_op jit(solution)/shard_map/ppermute | solution.py:18
  54.4 7.8 %collective-permute-start.10 = (f32[4,3,22,134]{3,0,2,1:T(4,128)S(1)}, f32[4,3,22,134]{3,0,2,1:T(4,128)S(1)}, u32[]{:S(2)}, u32[]{:S(2)}) collective-permute-start(f32[4,3,22,134]{3,0,2,1:T(4,128)S(1)} %get-tuple-element.30), channel_id=1, source_target_pairs={{0,1},{1,2},{2,3},{4,5},{5,6},{6,7},{8,9},{9,10},{10,11},{12,13},{... | collective-permute-start | bytes 424520 | tf_op jit(solution)/shard_map/ppermute | solution.py:17
  56.4 7.6 %collective-permute-start.11 = (f32[4,3,22,134]{3,0,2,1:T(4,128)S(1)}, f32[4,3,22,134]{3,0,2,1:T(4,128)S(1)}, u32[]{:S(2)}, u32[]{:S(2)}) collective-permute-start(f32[4,3,22,134]{3,0,2,1:T(4,128)S(1)} %get-tuple-element.31), channel_id=1, source_target_pairs={{1,0},{2,1},{3,2},{5,4},{6,5},{7,6},{9,8},{10,9},{11,10},{13,12},{... | collective-permute-start | bytes 424520 | tf_op jit(solution)/shard_map/ppermute | solution.py:18
  68.2 1.7 %copy-start.5 = (f32[4,16,128]{2,1,0:T(8,128)S(1)}, f32[4,16,128]{2,1,0:T(8,128)}, u32[]{:S(2)}) copy-start(f32[4,16,128]{2,1,0:T(8,128)} %param.16) | copy-start | bytes 98308
  69.8 0.7 copy-start.8
where the time goes:
time: 115 us
  blocking collectives  42.7 us (37%)
  starting transfers between devices  27.1 us (24%)
  waiting for transfers between devices  27 us (23%)
  other arithmetic  8.29 us (7%)
  local copies, waits for them, and re-layouts  5.05 us (4%)
  matrix products  3.69 us (3%)
    psum x1, blocking collectives, on_device(): total = lax.psum(terms, ('circ', 'normal', 'span'))  42.7 us
    ppermute x6, starting transfers between devices, padded_2(): after = lax.ppermute(initial, axis, down)  18.3 us
    ppermute x6, waiting for transfers between devices, padded_2(): after = lax.ppermute(initial, axis, down)  14.1 us
    ppermute x6, waiting for transfers between devices, padded_2(): before = lax.ppermute(last, axis, up)  12.9 us
    ppermute x6, starting transfers between devices, padded_2(): before = lax.ppermute(last, axis, up)  8.85 us
    mul x3, other arithmetic, relax(): weighted = stiff_pad[None] * mesh_pad  4.64 us
    unnamed x22, local copies, waits for them, and re-layouts  4.09 us
  transfers between devices with their start and end apart: 12, of which 11 were waited for; matrix products, arithmetic and copies ran while one was open for 1% of the time, Pallas kernels for 0%

commit v1 on v0

--- a/solution.py
+++ b/solution.py
@@ -102,7 +102,7 @@
         panel_owner[:, :, None] == jnp.arange(panel_count, dtype=jnp.int32)[None, None, :]
     ).astype(jnp.float32)
     terms = jnp.einsum("mki,kip->mp", wall_sens, onehot, precision=lax.Precision.HIGHEST)
-    total = lax.psum(terms, ("circ", "normal", "span"))
+    total = lax.psum(lax.psum(terms, ("normal", "span")), "circ")
     panels = lax.dynamic_slice_in_dim(total, lax.axis_index("span") * PANEL_DEV, PANEL_DEV, 1)
     return (residual, mesh, panels)
 

time: 115 us -> 102 us (0.89)
  the two profiles are of different devices: /device:TPU:14 before, /device:TPU:0 now
where the time goes in v1:
time: 102 us
  waiting for transfers between devices  31.3 us (31%)
  blocking collectives  28.5 us (28%)
  starting transfers between devices  23.9 us (23%)
  other arithmetic  8.29 us (8%)
  local copies, waits for them, and re-layouts  5.05 us (5%)
  matrix products  3.7 us (4%)
  between operations  1.06 us (1%)
    psum x2, blocking collectives, on_device(): total = lax.psum(lax.psum(terms, ('normal', 'span')), 'circ')  28.5 us
    ppermute x6, waiting for transfers between devices, padded_2(): after = lax.ppermute(initial, axis, down)  20.4 us
    ppermute x6, starting transfers between devices, padded_2(): before = lax.ppermute(last, axis, up)  13.8 us
    ppermute x6, waiting for transfers between devices, padded_2(): before = lax.ppermute(last, axis, up)  10.9 us
    ppermute x6, starting transfers between devices, padded_2(): after = lax.ppermute(initial, axis, down)  10.1 us
    mul x3, other arithmetic, relax(): weighted = stiff_pad[None] * mesh_pad  4.64 us
    unnamed x22, local copies, waits for them, and re-layouts  4.09 us
  transfers between devices with their start and end apart: 12, of which 10 were waited for; matrix products, arithmetic and copies ran while one was open for 1% of the time, Pallas kernels for 0%

profile of v1, /device:TPU:0, one launch (start us, length us, event | category | flops | bytes accessed | tf_op | source)
XLA Modules:
  0.0 101.8 jit_solution(8402697537194441990)
XLA Ops:
  0.7 1.0 constant_dynamic-update-slice_fusion.1
  1.8 3.1 %collective-permute-start = (f32[8,4,16,1]{3,2,1,0:T(8,128)S(1)}, f32[8,4,16,1]{3,2,1,0:T(8,128)S(1)}, u32[]{:S(2)}, u32[]{:S(2)}) collective-permute-start(f32[8,4,16,1]{3,2,1,0:T(8,128)S(1)} %get-tuple-element.32), channel_id=1, source_target_pairs={{0,8},{8,16},{16,24},{24,0},{1,9},{9,17},{17,25},{25,1},{2,10},{10... | collective-permute-start | bytes 6152 | tf_op jit(solution)/shard_map/ppermute | solution.py:17
  4.9 2.1 %collective-permute-start.1 = (f32[8,4,16,1]{3,2,1,0:T(8,128)S(1)}, f32[8,4,16,1]{3,2,1,0:T(8,128)S(1)}, u32[]{:S(2)}, u32[]{:S(2)}) collective-permute-start(f32[8,4,16,1]{3,2,1,0:T(8,128)S(1)} %get-tuple-element.33), channel_id=1, source_target_pairs={{8,0},{16,8},{24,16},{0,24},{9,1},{17,9},{25,17},{1,25},{10,2},{18... | collective-permute-start | bytes 6152 | tf_op jit(solution)/shard_map/ppermute | solution.py:18
  7.0 7.1 %collective-permute-done = f32[8,4,16,1]{3,2,1,0:T(8,128)S(1)} collective-permute-done((f32[8,4,16,1]{3,2,1,0:T(8,128)S(1)}, f32[8,4,16,1]{3,2,1,0:T(8,128)S(1)}, u32[]{:S(2)}, u32[]{:S(2)}) %collective-permute-start) | collective-permute-done | bytes 2080 | tf_op jit(solution)/shard_map/ppermute | solution.py:17
  14.1 4.2 %collective-permute-done.1 = f32[8,4,16,1]{3,2,1,0:T(8,128)S(1)} collective-permute-done((f32[8,4,16,1]{3,2,1,0:T(8,128)S(1)}, f32[8,4,16,1]{3,2,1,0:T(8,128)S(1)}, u32[]{:S(2)}, u32[]{:S(2)}) %collective-permute-start.1) | collective-permute-done | bytes 2080 | tf_op jit(solution)/shard_map/ppermute | solution.py:18
  18.5 3.4 %collective-permute-start.2 = (f32[8,4,1,130]{3,2,1,0:T(1,128)S(1)}, f32[8,4,1,130]{3,2,1,0:T(1,128)S(1)}, u32[]{:S(2)}, u32[]{:S(2)}) collective-permute-start(f32[8,4,1,130]{3,2,1,0:T(1,128)S(1)} %get-tuple-element.24), channel_id=1, source_target_pairs={{0,4},{1,5},{2,6},{3,7},{8,12},{9,13},{10,14},{11,15},{16,20},{17,... | collective-permute-start | bytes 49928 | tf_op jit(solution)/shard_map/ppermute | solution.py:17
  22.0 1.3 %collective-permute-start.3 = (f32[8,4,1,130]{3,2,1,0:T(1,128)S(1)}, f32[8,4,1,130]{3,2,1,0:T(1,128)S(1)}, u32[]{:S(2)}, u32[]{:S(2)}) collective-permute-start(f32[8,4,1,130]{3,2,1,0:T(1,128)S(1)} %get-tuple-element.25), channel_id=1, source_target_pairs={{4,0},{5,1},{6,2},{7,3},{12,8},{13,9},{14,10},{15,11},{20,16},{21,... | collective-permute-start | bytes 49928 | tf_op jit(solution)/shard_map/ppermute | solution.py:18
  23.5 4.2 %collective-permute-done.3 = f32[8,4,1,130]{3,2,1,0:T(1,128)S(1)} collective-permute-done((f32[8,4,1,130]{3,2,1,0:T(1,128)S(1)}, f32[8,4,1,130]{3,2,1,0:T(1,128)S(1)}, u32[]{:S(2)}, u32[]{:S(2)}) %collective-permute-start.3) | collective-permute-done | bytes 16672 | tf_op jit(solution)/shard_map/ppermute | solution.py:18
  28.0 1.3 %collective-permute-start.5 = (f32[8,1,18,130]{3,2,1,0:T(8,128)S(1)}, f32[8,1,18,130]{3,2,1,0:T(8,128)S(1)}, u32[]{:S(2)}, u32[]{:S(2)}) collective-permute-start(f32[8,1,18,130]{3,2,1,0:T(8,128)S(1)} %get-tuple-element.22), channel_id=1, source_target_pairs={{0,1},{1,2},{2,3},{4,5},{5,6},{6,7},{8,9},{9,10},{10,11},{12,13},{... | collective-permute-start | bytes 224648 | tf_op jit(solution)/shard_map/ppermute | solution.py:17
  29.3 1.3 %collective-permute-start.4 = (f32[8,1,18,130]{3,2,1,0:T(8,128)S(1)}, f32[8,1,18,130]{3,2,1,0:T(8,128)S(1)}, u32[]{:S(2)}, u32[]{:S(2)}) collective-permute-start(f32[8,1,18,130]{3,2,1,0:T(8,128)S(1)} %get-tuple-element.23), channel_id=1, source_target_pairs={{1,0},{2,1},{3,2},{5,4},{6,5},{7,6},{9,8},{10,9},{11,10},{13,12},{... | collective-permute-start | bytes 224648 | tf_op jit(solution)/shard_map/ppermute | solution.py:18
  30.6 3.7 %collective-permute-done.4 = f32[8,1,18,130]{3,2,1,0:T(8,128)S(1)} collective-permute-done((f32[8,1,18,130]{3,2,1,0:T(8,128)S(1)}, f32[8,1,18,130]{3,2,1,0:T(8,128)S(1)}, u32[]{:S(2)}, u32[]{:S(2)}) %collective-permute-start.4) | collective-permute-done | bytes 74912 | tf_op jit(solution)/shard_map/ppermute | solution.py:18
  40.3 1.2 %collective-permute-start.6 = (f32[4,4,16,3]{3,0,2,1:T(4,128)S(1)}, f32[4,4,16,3]{3,0,2,1:T(4,128)S(1)}, u32[]{:S(2)}, u32[]{:S(2)}) collective-permute-start(f32[4,4,16,3]{3,0,2,1:T(4,128)S(1)} %get-tuple-element.38), channel_id=1, source_target_pairs={{0,8},{8,16},{16,24},{24,0},{1,9},{9,17},{17,25},{25,1},{2,10},{10... | collective-permute-start | bytes 9224 | tf_op jit(solution)/shard_map/ppermute | solution.py:17
  41.5 2.7 %collective-permute-start.7 = (f32[4,4,16,3]{3,0,2,1:T(4,128)S(1)}, f32[4,4,16,3]{3,0,2,1:T(4,128)S(1)}, u32[]{:S(2)}, u32[]{:S(2)}) collective-permute-start(f32[4,4,16,3]{3,0,2,1:T(4,128)S(1)} %get-tuple-element.39), channel_id=1, source_target_pairs={{8,0},{16,8},{24,16},{0,24},{9,1},{17,9},{25,17},{1,25},{10,2},{18... | collective-permute-start | bytes 9224 | tf_op jit(solution)/shard_map/ppermute | solution.py:18
  44.2 3.1 %collective-permute-done.6 = f32[4,4,16,3]{3,0,2,1:T(4,128)S(1)} collective-permute-done((f32[4,4,16,3]{3,0,2,1:T(4,128)S(1)}, f32[4,4,16,3]{3,0,2,1:T(4,128)S(1)}, u32[]{:S(2)}, u32[]{:S(2)}) %collective-permute-start.6) | collective-permute-done | bytes 3104 | tf_op jit(solution)/shard_map/ppermute | solution.py:17
  48.1 1.6 %collective-permute-start.8 = (f32[4,4,3,134]{3,0,2,1:T(4,128)S(1)}, f32[4,4,3,134]{3,0,2,1:T(4,128)S(1)}, u32[]{:S(2)}, u32[]{:S(2)}) collective-permute-start(f32[4,4,3,134]{3,0,2,1:T(4,128)S(1)} %get-tuple-element.28), channel_id=1, source_target_pairs={{0,4},{1,5},{2,6},{3,7},{8,12},{9,13},{10,14},{11,15},{16,20},{17,... | collective-permute-start | bytes 77192 | tf_op jit(solution)/shard_map/ppermute | solution.py:17
  49.7 1.3 %collective-permute-start.9 = (f32[4,4,3,134]{3,0,2,1:T(4,128)S(1)}, f32[4,4,3,134]{3,0,2,1:T(4,128)S(1)}, u32[]{:S(2)}, u32[]{:S(2)}) collective-permute-start(f32[4,4,3,134]{3,0,2,1:T(4,128)S(1)} %get-tuple-element.29), channel_id=1, source_target_pairs={{4,0},{5,1},{6,2},{7,3},{12,8},{13,9},{14,10},{15,11},{20,16},{21,... | collective-permute-start | bytes 77192 | tf_op jit(solution)/shard_map/ppermute | solution.py:18
  51.4 4.3 %collective-permute-done.9 = f32[4,4,3,134]{3,0,2,1:T(4,128)S(1)} collective-permute-done((f32[4,4,3,134]{3,0,2,1:T(4,128)S(1)}, f32[4,4,3,134]{3,0,2,1:T(4,128)S(1)}, u32[]{:S(2)}, u32[]{:S(2)}) %collective-permute-start.9) | collective-permute-done | bytes 25760 | tf_op jit(solution)/shard_map/ppermute | solution.py:18
  56.2 3.2 %collective-permute-start.10 = (f32[4,3,22,134]{3,0,2,1:T(4,128)S(1)}, f32[4,3,22,134]{3,0,2,1:T(4,128)S(1)}, u32[]{:S(2)}, u32[]{:S(2)}) collective-permute-start(f32[4,3,22,134]{3,0,2,1:T(4,128)S(1)} %get-tuple-element.30), channel_id=1, source_target_pairs={{0,1},{1,2},{2,3},{4,5},{5,6},{6,7},{8,9},{9,10},{10,11},{12,13},{... | collective-permute-start | bytes 424520 | tf_op jit(solution)/shard_map/ppermute | solution.py:17
  59.4 1.5 %collective-permute-start.11 = (f32[4,3,22,134]{3,0,2,1:T(4,128)S(1)}, f32[4,3,22,134]{3,0,2,1:T(4,128)S(1)}, u32[]{:S(2)}, u32[]{:S(2)}) collective-permute-start(f32[4,3,22,134]{3,0,2,1:T(4,128)S(1)} %get-tuple-element.31), channel_id=1, source_target_pairs={{1,0},{2,1},{3,2},{5,4},{6,5},{7,6},{9,8},{10,9},{11,10},{13,12},{... | collective-permute-start | bytes 424520 | tf_op jit(solution)/shard_map/ppermute | solution.py:18
  61.6 3.4 %collective-permute-done.11 = f32[4,3,22,134]{3,0,2,1:T(4,128)S(1)} collective-permute-done((f32[4,3,22,134]{3,0,2,1:T(4,128)S(1)}, f32[4,3,22,134]{3,0,2,1:T(4,128)S(1)}, u32[]{:S(2)}, u32[]{:S(2)}) %collective-permute-start.11) | collective-permute-done | bytes 141536 | tf_op jit(solution)/shard_map/ppermute | solution.py:18
  66.8 2.4 %broadcast_multiply_fusion.1 = (f32[3,8,20,132]{3,0,2,1:T(4,128)S(1)}, f32[3,8,20,132]{3,0,2,1:T(4,128)S(1)}) fusion(f32[8,20,132]{2,1,0:T(8,128)S(1)} %get-tuple-element.37, f32[3,10,22,134]{3,0,2,1:T(4,128)S(1)} %get-tuple-element.12, f32[8,20,132]{2,1,0:T(8,128)S(1)} %get-tuple-element.36, f32[4,10,22,134]{3,0,2,1:T(4,128)S(1)} %pad_maximum_fusion, ...), kind=kLoop, calls=%fused_computation.35 | loop fusion | flops 760320 | bytes 2703360 | tf_op jit(solution)/shard_map/mul | solution.py:57
  69.2 1.7 %broadcast_multiply_fusion.2 = (f32[3,6,18,130]{3,0,2,1:T(4,128)S(1)}, f32[3,6,18,130]{3,0,2,1:T(4,128)S(1)}) fusion(f32[6,18,130]{2,1,0:T(8,128)S(1)} %get-tuple-element.35, f32[3,8,20,132]{3,0,2,1:T(4,128)S(1)} %get-tuple-element.10, f32[6,18,130]{2,1,0:T(8,128)S(1)} %get-tuple-element.34, f32[4,10,22,134]{3,0,2,1:T(4,128)S(1)} %pad_maximum_fusion, ...), kind=kLoop, calls=%fused_computation.46 | loop fusion | flops 505440 | bytes 1797120 | tf_op jit(solution)/shard_map/mul | solution.py:57
  72.1 16.9 %psum.14 = f32[3,512]{1,0:T(4,128)S(1)} all-reduce(f32[3,512]{1,0:T(4,128)S(1)} %convolution_bitcast_fusion.1), channel_id=1, replica_groups=mesh['circ'=4,'normal'=2,'span'=4] {'normal','span'}, use_global_device_ids=true, to_apply=%region_1.0 | all-reduce | flops 1536 | bytes 12288 | tf_op jit(solution)/shard_map/psum | solution.py:105
  88.9 11.6 %psum.15 = f32[3,512]{1,0:T(4,128)S(1)} all-reduce(f32[3,512]{1,0:T(4,128)S(1)} %psum.14), channel_id=1, replica_groups=mesh['circ'=4,'normal'=2,'span'=4] {'circ'}, use_global_device_ids=true, to_apply=%region_2.0 | all-reduce | flops 1536 | bytes 12288 | tf_op jit(solution)/shard_map/psum | solution.py:105
  (60 shorter events, 13.2 us)
Async XLA Ops:
  0.6 38.7 %copy-start = (f32[3,5]{1,0:T(4,128)S(1)}, f32[3,5]{1,0:T(4,128)}, u32[]{:S(2)}) copy-start(f32[3,5]{1,0:T(4,128)} %param.14) | copy-start | bytes 184
  0.6 1.0 copy-start.4
  1.8 12.3 %collective-permute-start = (f32[8,4,16,1]{3,2,1,0:T(8,128)S(1)}, f32[8,4,16,1]{3,2,1,0:T(8,128)S(1)}, u32[]{:S(2)}, u32[]{:S(2)}) collective-permute-start(f32[8,4,16,1]{3,2,1,0:T(8,128)S(1)} %get-tuple-element.32), channel_id=1, source_target_pairs={{0,8},{8,16},{16,24},{24,0},{1,9},{9,17},{17,25},{25,1},{2,10},{10... | collective-permute-start | bytes 6152 | tf_op jit(solution)/shard_map/ppermute | solution.py:17
  4.9 13.4 %collective-permute-start.1 = (f32[8,4,16,1]{3,2,1,0:T(8,128)S(1)}, f32[8,4,16,1]{3,2,1,0:T(8,128)S(1)}, u32[]{:S(2)}, u32[]{:S(2)}) collective-permute-start(f32[8,4,16,1]{3,2,1,0:T(8,128)S(1)} %get-tuple-element.33), channel_id=1, source_target_pairs={{8,0},{16,8},{24,16},{0,24},{9,1},{17,9},{25,17},{1,25},{10,2},{18... | collective-permute-start | bytes 6152 | tf_op jit(solution)/shard_map/ppermute | solution.py:18
  7.0 16.3 %copy-start.6 = (f32[3,5,5]{2,0,1:T(4,128)S(1)}, f32[3,5,5]{2,0,1:T(4,128)}, u32[]{:S(2)}) copy-start(f32[3,5,5]{2,0,1:T(4,128)} %param.12) | copy-start | bytes 904
  18.5 5.0 %collective-permute-start.2 = (f32[8,4,1,130]{3,2,1,0:T(1,128)S(1)}, f32[8,4,1,130]{3,2,1,0:T(1,128)S(1)}, u32[]{:S(2)}, u32[]{:S(2)}) collective-permute-start(f32[8,4,1,130]{3,2,1,0:T(1,128)S(1)} %get-tuple-element.24), channel_id=1, source_target_pairs={{0,4},{1,5},{2,6},{3,7},{8,12},{9,13},{10,14},{11,15},{16,20},{17,... | collective-permute-start | bytes 49928 | tf_op jit(solution)/shard_map/ppermute | solution.py:17
  22.0 5.8 %collective-permute-start.3 = (f32[8,4,1,130]{3,2,1,0:T(1,128)S(1)}, f32[8,4,1,130]{3,2,1,0:T(1,128)S(1)}, u32[]{:S(2)}, u32[]{:S(2)}) collective-permute-start(f32[8,4,1,130]{3,2,1,0:T(1,128)S(1)} %get-tuple-element.25), channel_id=1, source_target_pairs={{4,0},{5,1},{6,2},{7,3},{12,8},{13,9},{14,10},{15,11},{20,16},{21,... | collective-permute-start | bytes 49928 | tf_op jit(solution)/shard_map/ppermute | solution.py:18
  23.3 7.3 %copy-start.7 = (f32[3,5,5]{2,0,1:T(4,128)S(1)}, f32[3,5,5]{2,0,1:T(4,128)}, u32[]{:S(2)}) copy-start(f32[3,5,5]{2,0,1:T(4,128)} %param.13) | copy-start | bytes 904
  28.0 2.6 %collective-permute-start.5 = (f32[8,1,18,130]{3,2,1,0:T(8,128)S(1)}, f32[8,1,18,130]{3,2,1,0:T(8,128)S(1)}, u32[]{:S(2)}, u32[]{:S(2)}) collective-permute-start(f32[8,1,18,130]{3,2,1,0:T(8,128)S(1)} %get-tuple-element.22), channel_id=1, source_target_pairs={{0,1},{1,2},{2,3},{4,5},{5,6},{6,7},{8,9},{9,10},{10,11},{12,13},{... | collective-permute-start | bytes 224648 | tf_op jit(solution)/shard_map/ppermute | solution.py:17
  29.3 5.1 %collective-permute-start.4 = (f32[8,1,18,130]{3,2,1,0:T(8,128)S(1)}, f32[8,1,18,130]{3,2,1,0:T(8,128)S(1)}, u32[]{:S(2)}, u32[]{:S(2)}) collective-permute-start(f32[8,1,18,130]{3,2,1,0:T(8,128)S(1)} %get-tuple-element.23), channel_id=1, source_target_pairs={{1,0},{2,1},{3,2},{5,4},{6,5},{7,6},{9,8},{10,9},{11,10},{13,12},{... | collective-permute-start | bytes 224648 | tf_op jit(solution)/shard_map/ppermute | solution.py:18
  34.5 0.9 copy-start.1
  37.8 0.9 copy-start.3
  39.4 0.8 copy-start.2
  40.3 7.0 %collective-permute-start.6 = (f32[4,4,16,3]{3,0,2,1:T(4,128)S(1)}, f32[4,4,16,3]{3,0,2,1:T(4,128)S(1)}, u32[]{:S(2)}, u32[]{:S(2)}) collective-permute-start(f32[4,4,16,3]{3,0,2,1:T(4,128)S(1)} %get-tuple-element.38), channel_id=1, source_target_pairs={{0,8},{8,16},{16,24},{24,0},{1,9},{9,17},{17,25},{25,1},{2,10},{10... | collective-permute-start | bytes 9224 | tf_op jit(solution)/shard_map/ppermute | solution.py:17
  41.5 6.4 %collective-permute-start.7 = (f32[4,4,16,3]{3,0,2,1:T(4,128)S(1)}, f32[4,4,16,3]{3,0,2,1:T(4,128)S(1)}, u32[]{:S(2)}, u32[]{:S(2)}) collective-permute-start(f32[4,4,16,3]{3,0,2,1:T(4,128)S(1)} %get-tuple-element.39), channel_id=1, source_target_pairs={{8,0},{16,8},{24,16},{0,24},{9,1},{17,9},{25,17},{1,25},{10,2},{18... | collective-permute-start | bytes 9224 | tf_op jit(solution)/shard_map/ppermute | solution.py:18
  48.1 3.4 %collective-permute-start.8 = (f32[4,4,3,134]{3,0,2,1:T(4,128)S(1)}, f32[4,4,3,134]{3,0,2,1:T(4,128)S(1)}, u32[]{:S(2)}, u32[]{:S(2)}) collective-permute-start(f32[4,4,3,134]{3,0,2,1:T(4,128)S(1)} %get-tuple-element.28), channel_id=1, source_target_pairs={{0,4},{1,5},{2,6},{3,7},{8,12},{9,13},{10,14},{11,15},{16,20},{17,... | collective-permute-start | bytes 77192 | tf_op jit(solution)/shard_map/ppermute | solution.py:17
  49.7 6.0 %collective-permute-start.9 = (f32[4,4,3,134]{3,0,2,1:T(4,128)S(1)}, f32[4,4,3,134]{3,0,2,1:T(4,128)S(1)}, u32[]{:S(2)}, u32[]{:S(2)}) collective-permute-start(f32[4,4,3,134]{3,0,2,1:T(4,128)S(1)} %get-tuple-element.29), channel_id=1, source_target_pairs={{4,0},{5,1},{6,2},{7,3},{12,8},{13,9},{14,10},{15,11},{20,16},{21,... | collective-permute-start | bytes 77192 | tf_op jit(solution)/shard_map/ppermute | solution.py:18
  56.2 5.4 %collective-permute-start.10 = (f32[4,3,22,134]{3,0,2,1:T(4,128)S(1)}, f32[4,3,22,134]{3,0,2,1:T(4,128)S(1)}, u32[]{:S(2)}, u32[]{:S(2)}) collective-permute-start(f32[4,3,22,134]{3,0,2,1:T(4,128)S(1)} %get-tuple-element.30), channel_id=1, source_target_pairs={{0,1},{1,2},{2,3},{4,5},{5,6},{6,7},{8,9},{9,10},{10,11},{12,13},{... | collective-permute-start | bytes 424520 | tf_op jit(solution)/shard_map/ppermute | solution.py:17
  59.4 5.6 %collective-permute-start.11 = (f32[4,3,22,134]{3,0,2,1:T(4,128)S(1)}, f32[4,3,22,134]{3,0,2,1:T(4,128)S(1)}, u32[]{:S(2)}, u32[]{:S(2)}) collective-permute-start(f32[4,3,22,134]{3,0,2,1:T(4,128)S(1)} %get-tuple-element.31), channel_id=1, source_target_pairs={{1,0},{2,1},{3,2},{5,4},{6,5},{7,6},{9,8},{10,9},{11,10},{13,12},{... | collective-permute-start | bytes 424520 | tf_op jit(solution)/shard_map/ppermute | solution.py:18
  69.2 1.7 %copy-start.5 = (f32[4,16,128]{2,1,0:T(8,128)S(1)}, f32[4,16,128]{2,1,0:T(8,128)}, u32[]{:S(2)}) copy-start(f32[4,16,128]{2,1,0:T(8,128)} %param.16) | copy-start | bytes 98308
  70.9 0.7 copy-start.8
